TPU v7x, 256 devices: a whole 4x4x8 slice. The times are simulated.
256 devices in a mesh: ctx: 32 (over y_hi, z, core), uly: 8 (over x, y_lo).
Axes of the slice: x: 4, y: 4 (y_hi: 2, y_lo: 2; y = y_hi * 2 + y_lo), z: 8, core: 2. Of those that a mesh axis runs over, the one named last changes fastest.
Arguments:
- queries: bfloat16 [32768, 4096], P(('ctx', 'uly')), may hold values from -200 to 200, as said below
- keys: bfloat16 [32768, 1024], P(('ctx', 'uly')), may hold values from -6 to 6, as said below
- values: bfloat16 [32768, 1024], P(('ctx', 'uly')), may hold values from -6 to 6
Outputs:
- attended: bfloat16 [32768, 4096], P(('ctx', 'uly'))
Inputs may be any that keep to these rules, and one draw needn't show every extreme that they name: `queries`: entries of order one, except that some query rows may be large. `keys`: entries of order one.
All inputs are finite; a program needn't handle non-finite values.
Results may differ from a plain program's by a relative error of at most 0.0055.
Values may be sent and summed in bfloat16 or wider, within the bound.
No kernel may reach another device: no remote copies, remote signals or barrier semaphores. Data moves between devices by JAX's collectives and lax.ppermute only.
A program may use at most 64 MiB of HBM per device.

v0:
```python
import functools

import jax
import jax.numpy as jnp
from jax import lax
from jax.experimental import pallas as pl
from jax.experimental.pallas import tpu as pltpu
from jax.sharding import PartitionSpec as P


HEAD_SIZE = 128
WINDOW_BLOCKS = 3
KEY_TILE = 1024
LOG2_E = 1.4426950408889634
HEADS_PER_STEP = 2


def passed_along(block, axis, distance):
    devices = range(lax.axis_size(axis))
    route = [(i - distance, i) for i in devices if i - distance in devices]
    return lax.ppermute(block, axis, route)


def attend_kernel(pos_ref, q_ref, kv_ref, *refs, block_len, back, last, hps=1):
    if last:
        parts = [refs[3 * i:3 * i + 3] for i in range(WINDOW_BLOCKS)]
        o_ref = refs[3 * WINDOW_BLOCKS]
        m_ref, l_ref, acc_ref = refs[3 * WINDOW_BLOCKS + 1:]
    else:
        m_ref, l_ref, acc_ref = refs
    cycle_pos = pos_ref[0]
    exp_scale = HEAD_SIZE ** (-0.5) * LOG2_E
    tile = min(KEY_TILE, block_len)

    def process(start, masked, fresh, hh=0):
        q = q_ref[:, pl.ds(hh * HEAD_SIZE, HEAD_SIZE)]
        mr, lr, ar = (m_ref.at[hh], l_ref.at[hh], acc_ref.at[hh]) if not last else (m_ref, l_ref, acc_ref)
        return _process(q, mr, lr, ar, start, masked, fresh)

    def _process(q, m_ref, l_ref, acc_ref, start, masked, fresh):
        k = kv_ref[pl.ds(start, tile), pl.ds(0, HEAD_SIZE)]
        v = kv_ref[pl.ds(start, tile), pl.ds(HEAD_SIZE, HEAD_SIZE)]
        s = lax.dot_general(k, q, (((1,), (1,)), ((), ())), preferred_element_type=jnp.float32)
        if masked:
            keys = lax.broadcasted_iota(jnp.int32, s.shape, 0) + start
            rows = lax.broadcasted_iota(jnp.int32, s.shape, 1)
            s = jnp.where(keys <= rows, s, jnp.float32(-1e30))
        if fresh:
            m_new = jnp.max(s, axis=0, keepdims=True)
        else:
            m_old = m_ref[...]
            m_new = jnp.maximum(m_old, jnp.max(s, axis=0, keepdims=True))
        p = jnp.exp2((s - m_new) * exp_scale)
        pv = lax.dot_general(
            v, p.astype(jnp.bfloat16), (((0,), (0,)), ((), ())), preferred_element_type=jnp.float32
        )
        if fresh:
            l_ref[...] = jnp.sum(p, axis=0, keepdims=True)
            acc_ref[...] = pv
        else:
            factor = jnp.exp2((m_old - m_new) * exp_scale)
            l_ref[...] = l_ref[...] * factor + jnp.sum(p, axis=0, keepdims=True)
            acc_ref[...] = acc_ref[...] * factor + pv
        m_ref[...] = m_new

    starts = [t * tile for t in range(block_len // tile)]
    for hh in range(hps):
        for j, start in enumerate(starts):
            process(start, back == 0, j == 0, hh)

    if last:
        states = [(r[0][...], r[1][...], r[2][...]) for r in parts] + [(m_ref[...], l_ref[...], acc_ref[...])]
        seen = [cycle_pos >= b for b in range(len(states))]
        m_all = states[0][0]
        for b in range(1, len(states)):
            m_all = jnp.maximum(m_all, jnp.where(seen[b], states[b][0], -jnp.inf))
        total = jnp.zeros_like(m_all)
        acc = jnp.zeros(acc_ref.shape, jnp.float32)
        for b, (m_b, l_b, acc_b) in enumerate(states):
            factor = jnp.exp2((m_b - m_all) * exp_scale)
            total = total + jnp.where(seen[b], l_b * factor, 0.0)
            acc = acc + jnp.where(seen[b], acc_b * factor, 0.0)
        o_ref[...] = (acc / total).T.astype(o_ref.dtype)


def attend(pos, q_src, kv, kv_col, q_heads, back, parts=None):
    block_len = q_src.shape[0]
    last = parts is not None
    hps = 1 if last else HEADS_PER_STEP
    kernel = functools.partial(attend_kernel, block_len=block_len, back=back, last=last, hps=hps)
    row_spec = pl.BlockSpec((None, 1, block_len), lambda h, pos: (h, 0, 0))
    acc_spec = pl.BlockSpec((None, HEAD_SIZE, block_len), lambda h, pos: (h, 0, 0))
    if not last:
        row_spec = pl.BlockSpec((hps, 1, block_len), lambda h, pos: (h, 0, 0))
        acc_spec = pl.BlockSpec((hps, HEAD_SIZE, block_len), lambda h, pos: (h, 0, 0))
    in_specs = [
        pl.BlockSpec((block_len, hps * HEAD_SIZE), lambda h, pos: (0, h)),
        pl.BlockSpec((block_len, 2 * HEAD_SIZE), lambda h, pos: (0, kv_col)),
    ]
    operands = [pos, q_src, kv]
    state_shapes = [
        jax.ShapeDtypeStruct((q_heads, 1, block_len), jnp.float32),
        jax.ShapeDtypeStruct((q_heads, 1, block_len), jnp.float32),
        jax.ShapeDtypeStruct((q_heads, HEAD_SIZE, block_len), jnp.float32),
    ]
    if last:
        for part in parts:
            in_specs += [row_spec, row_spec, acc_spec]
            operands += list(part)
        out_specs = pl.BlockSpec((block_len, HEAD_SIZE), lambda h, pos: (0, h))
        out_shape = jax.ShapeDtypeStruct((block_len, q_heads * HEAD_SIZE), jnp.bfloat16)
        scratch = [
            pltpu.VMEM((1, block_len), jnp.float32),
            pltpu.VMEM((1, block_len), jnp.float32),
            pltpu.VMEM((HEAD_SIZE, block_len), jnp.float32),
        ]
    else:
        out_specs = [row_spec, row_spec, acc_spec]
        out_shape = state_shapes
        scratch = []
    grid_spec = pltpu.PrefetchScalarGridSpec(
        num_scalar_prefetch=1,
        grid=(q_heads // hps,),
        in_specs=in_specs,
        out_specs=out_specs,
        scratch_shapes=scratch,
    )
    return pl.pallas_call(
        kernel,
        grid_spec=grid_spec,
        out_shape=out_shape,
        compiler_params=pltpu.CompilerParams(dimension_semantics=("arbitrary",)),
    )(*operands)


def on_device(queries, keys, values):
    n = lax.axis_size("uly")
    rows = queries.shape[0]
    cycle_pos = lax.axis_index("ctx")
    packed = jnp.concatenate(
        [queries.reshape(rows, n, -1), keys.reshape(rows, n, -1), values.reshape(rows, n, -1)], axis=2
    )
    qkv = lax.all_to_all(packed, "uly", split_axis=1, concat_axis=0, tiled=True)
    qkv = qkv.reshape(rows * n, -1)
    q_heads = (qkv.shape[1] - 2 * HEAD_SIZE) // HEAD_SIZE
    pos = jnp.reshape(cycle_pos, (1,)).astype(jnp.int32)
    kv = qkv[:, q_heads * HEAD_SIZE:]
    parts = [attend(pos, qkv, qkv, q_heads // 2, q_heads, 0)]
    for back in range(1, WINDOW_BLOCKS + 1):
        kv = jnp.concatenate(
            [passed_along(kv[:, :HEAD_SIZE], "ctx", 1), passed_along(kv[:, HEAD_SIZE:], "ctx", 1)], axis=1
        )
        last = back == WINDOW_BLOCKS
        parts.append(attend(pos, qkv, kv, 0, q_heads, back, parts if last else None))
    return lax.all_to_all(parts[-1], "uly", split_axis=0, concat_axis=1, tiled=True)


def solution(mesh):
    placed = (P(("ctx", "uly"), None), P(("ctx", "uly"), None), P(("ctx", "uly"), None))
    return jax.shard_map(
        on_device, mesh=mesh, in_specs=placed, out_specs=P(("ctx", "uly"), None), check_vma=False
    )
```

profile of v0, /device:TPU:224, one launch (start us, length us, event | category | flops | bytes accessed | tf_op | source)
XLA Modules:
  0.0 111.0 jit_solution(13172075005316222175)
XLA Ops:
  0.0 0.0 copy-start
  0.0 0.0 copy-start.2
  0.0 1.4 %copy.15 = bf16[16,8,8,512]{3,2,0,1:T(8,128)(2,1)S(1)} copy(bf16[16,8,8,512]{3,2,1,0:T(8,128)(2,1)} %bitcast.33) | data formatting | bytes 2097152 | tf_op jit(solution)/shard_map/reshape | solution.py:141
  1.4 0.0 copy-done
  1.4 0.0 copy-done.2
  1.4 0.1 copy_bitcast_fusion.1
  1.5 0.1 pad_maximum_fusion
  1.7 26.1 %all_to_all.34 = bf16[128,8,768]{2,0,1:T(8,128)(2,1)S(1)} all-to-all(bf16[128,8,768]{2,0,1:T(8,128)(2,1)S(1)} %pad_maximum_fusion), channel_id=1, replica_groups=mesh['ctx'=32,'uly'=8] {'uly'}, dimensions={1} | all-to-all | bytes 3145728 | tf_op jit(solution)/shard_map/all_to_all | solution.py:143
  27.7 0.0 copy-start.1
  27.8 1.9 %collective-permute-start = (bf16[1024,128]{1,0:T(8,128)(2,1)S(1)}, bf16[1024,128]{1,0:T(8,128)(2,1)S(1)}, u32[]{:S(2)}, u32[]{:S(2)}) collective-permute-start(bf16[1024,128]{1,0:T(8,128)(2,1)S(1)} %get-tuple-element.23), channel_id=1, source_target_pairs={{0,8},{8,16},{16,24},{24,32},{32,40},{40,48},{48,56},{56,64},{64,7... | collective-permute-start | bytes 786440 | tf_op jit(solution)/shard_map/ppermute | solution.py:21
  29.7 1.9 %collective-permute-start.3 = (bf16[1024,128]{1,0:T(8,128)(2,1)S(1)}, bf16[1024,128]{1,0:T(8,128)(2,1)S(1)}, u32[]{:S(2)}, u32[]{:S(2)}) collective-permute-start(bf16[1024,128]{1,0:T(8,128)(2,1)S(1)} %get-tuple-element.24), channel_id=1, source_target_pairs={{0,8},{8,16},{16,24},{24,32},{32,40},{40,48},{48,56},{56,64},{64,7... | collective-permute-start | bytes 786440 | tf_op jit(solution)/shard_map/ppermute | solution.py:21
  31.6 3.8 %collective-permute-done = bf16[1024,128]{1,0:T(8,128)(2,1)S(1)} collective-permute-done((bf16[1024,128]{1,0:T(8,128)(2,1)S(1)}, bf16[1024,128]{1,0:T(8,128)(2,1)S(1)}, u32[]{:S(2)}, u32[]{:S(2)}) %collective-permute-start) | collective-permute-done | bytes 262176 | tf_op jit(solution)/shard_map/ppermute | solution.py:21
  35.5 1.9 %collective-permute-start.1 = (bf16[1024,128]{1,0:T(8,128)(2,1)S(1)}, bf16[1024,128]{1,0:T(8,128)(2,1)S(1)}, u32[]{:S(2)}, u32[]{:S(2)}) collective-permute-start(bf16[1024,128]{1,0:T(8,128)(2,1)S(1)} %collective-permute-done), channel_id=1, source_target_pairs={{0,8},{8,16},{16,24},{24,32},{32,40},{40,48},{48,56},{56,64},{64,7... | collective-permute-start | bytes 786440 | tf_op jit(solution)/shard_map/ppermute | solution.py:21
  37.4 0.9 collective-permute-done.3
  38.3 4.5 %collective-permute-start.4 = (bf16[1024,128]{1,0:T(8,128)(2,1)S(1)}, bf16[1024,128]{1,0:T(8,128)(2,1)S(1)}, u32[]{:S(2)}, u32[]{:S(2)}) collective-permute-start(bf16[1024,128]{1,0:T(8,128)(2,1)S(1)} %collective-permute-done.3), channel_id=1, source_target_pairs={{0,8},{8,16},{16,24},{24,32},{32,40},{40,48},{48,56},{56,64},{64,7... | collective-permute-start | bytes 786440 | tf_op jit(solution)/shard_map/ppermute | solution.py:21
  42.8 0.4 collective-permute-done.1
  43.2 2.9 %collective-permute-start.2 = (bf16[1024,128]{1,0:T(8,128)(2,1)S(1)}, bf16[1024,128]{1,0:T(8,128)(2,1)S(1)}, u32[]{:S(2)}, u32[]{:S(2)}) collective-permute-start(bf16[1024,128]{1,0:T(8,128)(2,1)S(1)} %collective-permute-done.1), channel_id=1, source_target_pairs={{0,8},{8,16},{16,24},{24,32},{32,40},{40,48},{48,56},{56,64},{64,7... | collective-permute-start | bytes 786440 | tf_op jit(solution)/shard_map/ppermute | solution.py:21
  46.0 0.0 collective-permute-done.4
  46.0 8.0 %collective-permute-start.5 = (bf16[1024,128]{1,0:T(8,128)(2,1)S(1)}, bf16[1024,128]{1,0:T(8,128)(2,1)S(1)}, u32[]{:S(2)}, u32[]{:S(2)}) collective-permute-start(bf16[1024,128]{1,0:T(8,128)(2,1)S(1)} %collective-permute-done.4), channel_id=1, source_target_pairs={{0,8},{8,16},{16,24},{24,32},{32,40},{40,48},{48,56},{56,64},{64,7... | collective-permute-start | bytes 786440 | tf_op jit(solution)/shard_map/ppermute | solution.py:21
  54.1 0.0 copy-done.1
  54.1 7.0 %shard_map.37 = (f32[4,1,1024]{2,1,0:T(1,128)}, f32[4,1,1024]{2,1,0:T(1,128)}, f32[4,128,1024]{2,1,0:T(8,128)}) custom-call(s32[1]{0:T(128)} %bitcast.pos_ref, bf16[1024,768]{1,0:T(8,128)(2,1)} %bitcast.25, bf16[1024,768]{1,0:T(8,128)(2,1)} %bitcast.26), custom_call_target="tpu_custom_call" | custom-call | tf_op jit(solution)/shard_map/pallas_call | solution.py:128
  61.0 0.8 pad_maximum_fusion.2.kv_ref
  61.9 8.0 %shard_map.38 = (f32[4,1,1024]{2,1,0:T(1,128)}, f32[4,1,1024]{2,1,0:T(1,128)}, f32[4,128,1024]{2,1,0:T(8,128)}) custom-call(s32[1]{0:T(128)} %bitcast.pos_ref, bf16[1024,768]{1,0:T(8,128)(2,1)} %bitcast.27, bf16[1024,256]{1,0:T(8,128)(2,1)} %pad_maximum_fusion.2.kv_ref), custom_call_target="tpu_custom_call" | custom-call | tf_op jit(solution)/shard_map/pallas_call | solution.py:128
  69.9 0.8 pad_maximum_fusion.3.kv_ref
  70.7 8.0 %shard_map.39 = (f32[4,1,1024]{2,1,0:T(1,128)}, f32[4,1,1024]{2,1,0:T(1,128)}, f32[4,128,1024]{2,1,0:T(8,128)}) custom-call(s32[1]{0:T(128)} %bitcast.pos_ref, bf16[1024,768]{1,0:T(8,128)(2,1)} %bitcast.28, bf16[1024,256]{1,0:T(8,128)(2,1)} %pad_maximum_fusion.3.kv_ref), custom_call_target="tpu_custom_call" | custom-call | tf_op jit(solution)/shard_map/pallas_call | solution.py:128
  78.7 0.0 collective-permute-done.2
  78.7 0.0 collective-permute-done.5
  78.7 0.9 pad_maximum_fusion.1.kv_ref
  79.6 10.2 %shard_map.40 = bf16[1024,512]{1,0:T(8,128)(2,1)} custom-call(s32[1]{0:T(128)} %bitcast.pos_ref, bf16[1024,768]{1,0:T(8,128)(2,1)} %bitcast.29, bf16[1024,256]{1,0:T(8,128)(2,1)} %pad_maximum_fusion.1.kv_ref, f32[4,1,1024]{2,1,0:T(1,128)} %get-tuple-element.14.refs_0_, f32[4,1,1024]{2,1,0:T(1,128)} %get-tuple-element.15.refs_1_, ...), custom_call_target="tpu_custom_call" | custom-call | tf_op jit(solution)/shard_map/pallas_call | solution.py:128
  89.8 20.1 %all_to_all.35 = bf16[8,128,512]{2,1,0:T(8,128)(2,1)S(1)} all-to-all(bf16[8,128,512]{2,1,0:T(8,128)(2,1)} %bitcast.30), channel_id=1, replica_groups=mesh['ctx'=32,'uly'=8] {'uly'}, dimensions={0} | all-to-all | bytes 2097152 | tf_op jit(solution)/shard_map/all_to_all | solution.py:155
  109.9 1.1 copy.11
  (1 shorter events, 0.0 us)
Async XLA Ops:
  0.0 1.4 %copy-start = (bf16[128,1024]{1,0:T(8,128)(2,1)S(1)}, bf16[128,1024]{1,0:T(8,128)(2,1)}, u32[]{:S(2)}) copy-start(bf16[128,1024]{1,0:T(8,128)(2,1)} %param.4) | copy-start | bytes 786436
  0.0 1.4 %copy-start.2 = (bf16[128,1024]{1,0:T(8,128)(2,1)S(1)}, bf16[128,1024]{1,0:T(8,128)(2,1)}, u32[]{:S(2)}) copy-start(bf16[128,1024]{1,0:T(8,128)(2,1)} %param.5) | copy-start | bytes 786436
  27.7 26.3 %copy-start.1 = (bf16[128,8,768]{2,0,1:T(8,128)(2,1)}, bf16[128,8,768]{2,0,1:T(8,128)(2,1)S(1)}, u32[]{:S(2)}) copy-start(bf16[128,8,768]{2,0,1:T(8,128)(2,1)S(1)} %all_to_all.34) | copy-start | bytes 4718596
  27.8 7.7 %collective-permute-start = (bf16[1024,128]{1,0:T(8,128)(2,1)S(1)}, bf16[1024,128]{1,0:T(8,128)(2,1)S(1)}, u32[]{:S(2)}, u32[]{:S(2)}) collective-permute-start(bf16[1024,128]{1,0:T(8,128)(2,1)S(1)} %get-tuple-element.23), channel_id=1, source_target_pairs={{0,8},{8,16},{16,24},{24,32},{32,40},{40,48},{48,56},{56,64},{64,7... | collective-permute-start | bytes 786440 | tf_op jit(solution)/shard_map/ppermute | solution.py:21
  29.7 8.6 %collective-permute-start.3 = (bf16[1024,128]{1,0:T(8,128)(2,1)S(1)}, bf16[1024,128]{1,0:T(8,128)(2,1)S(1)}, u32[]{:S(2)}, u32[]{:S(2)}) collective-permute-start(bf16[1024,128]{1,0:T(8,128)(2,1)S(1)} %get-tuple-element.24), channel_id=1, source_target_pairs={{0,8},{8,16},{16,24},{24,32},{32,40},{40,48},{48,56},{56,64},{64,7... | collective-permute-start | bytes 786440 | tf_op jit(solution)/shard_map/ppermute | solution.py:21
  35.5 7.7 %collective-permute-start.1 = (bf16[1024,128]{1,0:T(8,128)(2,1)S(1)}, bf16[1024,128]{1,0:T(8,128)(2,1)S(1)}, u32[]{:S(2)}, u32[]{:S(2)}) collective-permute-start(bf16[1024,128]{1,0:T(8,128)(2,1)S(1)} %collective-permute-done), channel_id=1, source_target_pairs={{0,8},{8,16},{16,24},{24,32},{32,40},{40,48},{48,56},{56,64},{64,7... | collective-permute-start | bytes 786440 | tf_op jit(solution)/shard_map/ppermute | solution.py:21
  38.3 7.7 %collective-permute-start.4 = (bf16[1024,128]{1,0:T(8,128)(2,1)S(1)}, bf16[1024,128]{1,0:T(8,128)(2,1)S(1)}, u32[]{:S(2)}, u32[]{:S(2)}) collective-permute-start(bf16[1024,128]{1,0:T(8,128)(2,1)S(1)} %collective-permute-done.3), channel_id=1, source_target_pairs={{0,8},{8,16},{16,24},{24,32},{32,40},{40,48},{48,56},{56,64},{64,7... | collective-permute-start | bytes 786440 | tf_op jit(solution)/shard_map/ppermute | solution.py:21
  43.2 35.6 %collective-permute-start.2 = (bf16[1024,128]{1,0:T(8,128)(2,1)S(1)}, bf16[1024,128]{1,0:T(8,128)(2,1)S(1)}, u32[]{:S(2)}, u32[]{:S(2)}) collective-permute-start(bf16[1024,128]{1,0:T(8,128)(2,1)S(1)} %collective-permute-done.1), channel_id=1, source_target_pairs={{0,8},{8,16},{16,24},{24,32},{32,40},{40,48},{48,56},{56,64},{64,7... | collective-permute-start | bytes 786440 | tf_op jit(solution)/shard_map/ppermute | solution.py:21
  46.0 32.7 %collective-permute-start.5 = (bf16[1024,128]{1,0:T(8,128)(2,1)S(1)}, bf16[1024,128]{1,0:T(8,128)(2,1)S(1)}, u32[]{:S(2)}, u32[]{:S(2)}) collective-permute-start(bf16[1024,128]{1,0:T(8,128)(2,1)S(1)} %collective-permute-done.4), channel_id=1, source_target_pairs={{0,8},{8,16},{16,24},{24,32},{32,40},{40,48},{48,56},{56,64},{64,7... | collective-permute-start | bytes 786440 | tf_op jit(solution)/shard_map/ppermute | solution.py:21
where the time goes:
time: 112 us; the launch traced here: 111 us
  blocking collectives  46.2 us (41%)
  Pallas kernels  33.1 us (30%)
  starting transfers between devices  21.1 us (19%)
  waiting for transfers between devices  5.14 us (5%)
  other arithmetic  2.73 us (2%)
  local copies, waits for them, and re-layouts  2.61 us (2%)
    pallas_call x4, Pallas kernels, attend(): pl.pallas_call(kernel, grid_spec=grid_spec, out_shape=out_shape, compiler...  33.1 us
    all_to_all x1, blocking collectives, on_device(): qkv = lax.all_to_all(packed, 'uly', split_axis=1, concat_axis=0, tiled=True)  26.1 us
    ppermute x6, starting transfers between devices, passed_along(): return lax.ppermute(block, axis, route)  21.1 us
    all_to_all x1, blocking collectives, on_device(): lax.all_to_all(parts[-1], 'uly', split_axis=0, concat_axis=1, tiled=True)  20.1 us
    ppermute x6, waiting for transfers between devices, passed_along(): return lax.ppermute(block, axis, route)  5.14 us
    concatenate x3, other arithmetic, on_device(): jnp.concatenate([passed_along(kv[:, :HEAD_SIZE], 'ctx', 1), passed_along(...  2.59 us
  transfers between devices with their start and end apart: 6, of which 3 were waited for; matrix products, arithmetic and copies ran while one was open for 2% of the time, Pallas kernels for 21%

commit v1 on v0

--- a/solution.py
+++ b/solution.py
@@ -34,7 +34,7 @@
 
     def process(start, masked, fresh, hh=0):
         q = q_ref[:, pl.ds(hh * HEAD_SIZE, HEAD_SIZE)]
-        mr, lr, ar = (m_ref.at[hh], l_ref.at[hh], acc_ref.at[hh]) if not last else (m_ref, l_ref, acc_ref)
+        mr, lr, ar = m_ref.at[hh], l_ref.at[hh], acc_ref.at[hh]
         return _process(q, mr, lr, ar, start, masked, fresh)
 
     def _process(q, m_ref, l_ref, acc_ref, start, masked, fresh):
@@ -69,30 +69,28 @@
             process(start, back == 0, j == 0, hh)
 
     if last:
-        states = [(r[0][...], r[1][...], r[2][...]) for r in parts] + [(m_ref[...], l_ref[...], acc_ref[...])]
-        seen = [cycle_pos >= b for b in range(len(states))]
-        m_all = states[0][0]
-        for b in range(1, len(states)):
-            m_all = jnp.maximum(m_all, jnp.where(seen[b], states[b][0], -jnp.inf))
-        total = jnp.zeros_like(m_all)
-        acc = jnp.zeros(acc_ref.shape, jnp.float32)
-        for b, (m_b, l_b, acc_b) in enumerate(states):
-            factor = jnp.exp2((m_b - m_all) * exp_scale)
-            total = total + jnp.where(seen[b], l_b * factor, 0.0)
-            acc = acc + jnp.where(seen[b], acc_b * factor, 0.0)
-        o_ref[...] = (acc / total).T.astype(o_ref.dtype)
+        seen = [cycle_pos >= b for b in range(WINDOW_BLOCKS + 1)]
+        for hh in range(hps):
+            states = [(r[0][hh], r[1][hh], r[2][hh]) for r in parts] + [(m_ref[hh], l_ref[hh], acc_ref[hh])]
+            m_all = states[0][0]
+            for b in range(1, len(states)):
+                m_all = jnp.maximum(m_all, jnp.where(seen[b], states[b][0], -jnp.inf))
+            total = jnp.zeros_like(m_all)
+            acc = jnp.zeros(acc_ref.shape[1:], jnp.float32)
+            for b, (m_b, l_b, acc_b) in enumerate(states):
+                factor = jnp.exp2((m_b - m_all) * exp_scale)
+                total = total + jnp.where(seen[b], l_b * factor, 0.0)
+                acc = acc + jnp.where(seen[b], acc_b * factor, 0.0)
+            o_ref[:, pl.ds(hh * HEAD_SIZE, HEAD_SIZE)] = (acc / total).T.astype(o_ref.dtype)
 
 
 def attend(pos, q_src, kv, kv_col, q_heads, back, parts=None):
     block_len = q_src.shape[0]
     last = parts is not None
-    hps = 1 if last else HEADS_PER_STEP
+    hps = HEADS_PER_STEP
     kernel = functools.partial(attend_kernel, block_len=block_len, back=back, last=last, hps=hps)
-    row_spec = pl.BlockSpec((None, 1, block_len), lambda h, pos: (h, 0, 0))
-    acc_spec = pl.BlockSpec((None, HEAD_SIZE, block_len), lambda h, pos: (h, 0, 0))
-    if not last:
-        row_spec = pl.BlockSpec((hps, 1, block_len), lambda h, pos: (h, 0, 0))
-        acc_spec = pl.BlockSpec((hps, HEAD_SIZE, block_len), lambda h, pos: (h, 0, 0))
+    row_spec = pl.BlockSpec((hps, 1, block_len), lambda h, pos: (h, 0, 0))
+    acc_spec = pl.BlockSpec((hps, HEAD_SIZE, block_len), lambda h, pos: (h, 0, 0))
     in_specs = [
         pl.BlockSpec((block_len, hps * HEAD_SIZE), lambda h, pos: (0, h)),
         pl.BlockSpec((block_len, 2 * HEAD_SIZE), lambda h, pos: (0, kv_col)),
@@ -107,12 +105,12 @@
         for part in parts:
             in_specs += [row_spec, row_spec, acc_spec]
             operands += list(part)
-        out_specs = pl.BlockSpec((block_len, HEAD_SIZE), lambda h, pos: (0, h))
+        out_specs = pl.BlockSpec((block_len, hps * HEAD_SIZE), lambda h, pos: (0, h))
         out_shape = jax.ShapeDtypeStruct((block_len, q_heads * HEAD_SIZE), jnp.bfloat16)
         scratch = [
-            pltpu.VMEM((1, block_len), jnp.float32),
-            pltpu.VMEM((1, block_len), jnp.float32),
-            pltpu.VMEM((HEAD_SIZE, block_len), jnp.float32),
+            pltpu.VMEM((hps, 1, block_len), jnp.float32),
+            pltpu.VMEM((hps, 1, block_len), jnp.float32),
+            pltpu.VMEM((hps, HEAD_SIZE, block_len), jnp.float32),
         ]
     else:
         out_specs = [row_spec, row_spec, acc_spec]
@@ -147,9 +145,7 @@
     kv = qkv[:, q_heads * HEAD_SIZE:]
     parts = [attend(pos, qkv, qkv, q_heads // 2, q_heads, 0)]
     for back in range(1, WINDOW_BLOCKS + 1):
-        kv = jnp.concatenate(
-            [passed_along(kv[:, :HEAD_SIZE], "ctx", 1), passed_along(kv[:, HEAD_SIZE:], "ctx", 1)], axis=1
-        )
+        kv = passed_along(kv, "ctx", 1)
         last = back == WINDOW_BLOCKS
         parts.append(attend(pos, qkv, kv, 0, q_heads, back, parts if last else None))
     return lax.all_to_all(parts[-1], "uly", split_axis=0, concat_axis=1, tiled=True)

time: 112 us -> 109 us (0.973)
  the two profiles are of different devices: /device:TPU:224 before, /device:TPU:97 now
where the time goes in v1:
time: 109 us
  blocking collectives  41.3 us (38%)
  Pallas kernels  33.7 us (31%)
  starting transfers between devices  17.7 us (16%)
  waiting for transfers between devices  12.2 us (11%)
  local copies, waits for them, and re-layouts  3.46 us (3%)
    pallas_call x4, Pallas kernels, attend(): pl.pallas_call(kernel, grid_spec=grid_spec, out_shape=out_shape, compiler...  33.7 us
    all_to_all x1, blocking collectives, on_device(): qkv = lax.all_to_all(packed, 'uly', split_axis=1, concat_axis=0, tiled=True)  24.9 us
    ppermute x3, starting transfers between devices, passed_along(): return lax.ppermute(block, axis, route)  17.7 us
    all_to_all x1, blocking collectives, on_device(): lax.all_to_all(parts[-1], 'uly', split_axis=0, concat_axis=1, tiled=True)  16.4 us
    ppermute x3, waiting for transfers between devices, passed_along(): return lax.ppermute(block, axis, route)  12.2 us
  transfers between devices with their start and end apart: 3, of which 2 were waited for; matrix products, arithmetic and copies ran while one was open for 0% of the time, Pallas kernels for 21%

profile of v1, /device:TPU:97, one launch (start us, length us, event | category | flops | bytes accessed | tf_op | source)
XLA Modules:
  0.0 108.5 jit_solution(6237473427058120848)
XLA Ops:
  0.0 0.0 copy-start
  0.0 0.0 copy-start.5
  0.0 1.4 %copy.15 = bf16[16,8,8,512]{3,2,0,1:T(8,128)(2,1)S(1)} copy(bf16[16,8,8,512]{3,2,1,0:T(8,128)(2,1)} %bitcast.33) | data formatting | bytes 2097152 | tf_op jit(solution)/shard_map/reshape | solution.py:139
  1.4 0.0 copy-done
  1.4 0.0 copy-done.5
  1.4 0.1 copy_bitcast_fusion.1
  1.5 0.1 pad_maximum_fusion
  1.7 24.9 %all_to_all.34 = bf16[128,8,768]{2,0,1:T(8,128)(2,1)S(1)} all-to-all(bf16[128,8,768]{2,0,1:T(8,128)(2,1)S(1)} %pad_maximum_fusion), channel_id=1, replica_groups=mesh['ctx'=32,'uly'=8] {'uly'}, dimensions={1} | all-to-all | bytes 3145728 | tf_op jit(solution)/shard_map/all_to_all | solution.py:141
  26.6 0.0 copy-start.1
  26.6 6.5 %collective-permute-start = (bf16[1024,256]{1,0:T(8,128)(2,1)S(1)}, bf16[1024,256]{1,0:T(8,128)(2,1)S(1)}, u32[]{:S(2)}, u32[]{:S(2)}) collective-permute-start(bf16[1024,256]{1,0:T(8,128)(2,1)S(1)} %slice.4), channel_id=1, source_target_pairs={{0,8},{8,16},{16,24},{24,32},{32,40},{40,48},{48,56},{56,64},{64,7... | collective-permute-start | bytes 1572872 | tf_op jit(solution)/shard_map/ppermute | solution.py:21
  33.1 6.1 %collective-permute-done.kv_ref = bf16[1024,256]{1,0:T(8,128)(2,1)S(1)} collective-permute-done((bf16[1024,256]{1,0:T(8,128)(2,1)S(1)}, bf16[1024,256]{1,0:T(8,128)(2,1)S(1)}, u32[]{:S(2)}, u32[]{:S(2)}) %collective-permute-start) | collective-permute-done | bytes 524320 | tf_op jit(solution)/shard_map/ppermute | solution.py:21
  39.2 0.0 copy-start.2
  39.2 5.6 %collective-permute-start.1 = (bf16[1024,256]{1,0:T(8,128)(2,1)S(1)}, bf16[1024,256]{1,0:T(8,128)(2,1)S(1)}, u32[]{:S(2)}, u32[]{:S(2)}) collective-permute-start(bf16[1024,256]{1,0:T(8,128)(2,1)S(1)} %collective-permute-done.kv_ref), channel_id=1, source_target_pairs={{0,8},{8,16},{16,24},{24,32},{32,40},{40,48},{48,56},{56,64},{64,7... | collective-permute-start | bytes 1572872 | tf_op jit(solution)/shard_map/ppermute | solution.py:21
  44.8 6.1 %collective-permute-done.1.kv_ref = bf16[1024,256]{1,0:T(8,128)(2,1)S(1)} collective-permute-done((bf16[1024,256]{1,0:T(8,128)(2,1)S(1)}, bf16[1024,256]{1,0:T(8,128)(2,1)S(1)}, u32[]{:S(2)}, u32[]{:S(2)}) %collective-permute-start.1) | collective-permute-done | bytes 524320 | tf_op jit(solution)/shard_map/ppermute | solution.py:21
  50.9 0.0 copy-start.4
  50.9 5.6 %collective-permute-start.2 = (bf16[1024,256]{1,0:T(8,128)(2,1)S(1)}, bf16[1024,256]{1,0:T(8,128)(2,1)S(1)}, u32[]{:S(2)}, u32[]{:S(2)}) collective-permute-start(bf16[1024,256]{1,0:T(8,128)(2,1)S(1)} %collective-permute-done.1.kv_ref), channel_id=1, source_target_pairs={{0,8},{8,16},{16,24},{24,32},{32,40},{40,48},{48,56},{56,64},{64,7... | collective-permute-start | bytes 1572872 | tf_op jit(solution)/shard_map/ppermute | solution.py:21
  56.5 0.0 copy-done.1
  56.5 7.0 %shard_map.37 = (f32[4,1,1024]{2,1,0:T(1,128)}, f32[4,1,1024]{2,1,0:T(1,128)}, f32[4,128,1024]{2,1,0:T(8,128)}) custom-call(s32[1]{0:T(128)} %bitcast.pos_ref, bf16[1024,768]{1,0:T(8,128)(2,1)} %bitcast.25, bf16[1024,768]{1,0:T(8,128)(2,1)} %bitcast.26), custom_call_target="tpu_custom_call" | custom-call | tf_op jit(solution)/shard_map/pallas_call | solution.py:126
  63.5 0.0 copy-done.2
  63.5 8.0 %shard_map.38 = (f32[4,1,1024]{2,1,0:T(1,128)}, f32[4,1,1024]{2,1,0:T(1,128)}, f32[4,128,1024]{2,1,0:T(8,128)}) custom-call(s32[1]{0:T(128)} %bitcast.pos_ref, bf16[1024,768]{1,0:T(8,128)(2,1)} %bitcast.27, bf16[1024,256]{1,0:T(8,128)(2,1)} %copy-done.2), custom_call_target="tpu_custom_call" | custom-call | tf_op jit(solution)/shard_map/pallas_call | solution.py:126
  71.5 0.0 copy-done.4
  71.5 8.0 %shard_map.39 = (f32[4,1,1024]{2,1,0:T(1,128)}, f32[4,1,1024]{2,1,0:T(1,128)}, f32[4,128,1024]{2,1,0:T(8,128)}) custom-call(s32[1]{0:T(128)} %bitcast.pos_ref, bf16[1024,768]{1,0:T(8,128)(2,1)} %bitcast.28, bf16[1024,256]{1,0:T(8,128)(2,1)} %copy-done.4), custom_call_target="tpu_custom_call" | custom-call | tf_op jit(solution)/shard_map/pallas_call | solution.py:126
  79.5 0.0 collective-permute-done.2.kv_ref
  79.5 0.0 copy-start.3
  79.5 0.8 copy-done.3
  80.4 10.7 %shard_map.40 = bf16[1024,512]{1,0:T(8,128)(2,1)} custom-call(s32[1]{0:T(128)} %bitcast.pos_ref, bf16[1024,768]{1,0:T(8,128)(2,1)} %bitcast.29, bf16[1024,256]{1,0:T(8,128)(2,1)} %copy-done.3, f32[4,1,1024]{2,1,0:T(1,128)} %get-tuple-element.14.refs_0_, f32[4,1,1024]{2,1,0:T(1,128)} %get-tuple-element.15.refs_1_, f32[4,128,1024]{2,1,0:T(8,128)} %get-tuple-element.16.refs_2_, ...), custom_call_target="tpu_custom_call" | custom-call | tf_op jit(solution)/shard_map/pallas_call | solution.py:126
  91.1 16.4 %all_to_all.35 = bf16[8,128,512]{2,1,0:T(8,128)(2,1)S(1)} all-to-all(bf16[8,128,512]{2,1,0:T(8,128)(2,1)} %bitcast.30), channel_id=1, replica_groups=mesh['ctx'=32,'uly'=8] {'uly'}, dimensions={0} | all-to-all | bytes 2097152 | tf_op jit(solution)/shard_map/all_to_all | solution.py:151
  107.5 1.1 copy.11
  (1 shorter events, 0.0 us)
Async XLA Ops:
  0.0 1.4 %copy-start = (bf16[128,1024]{1,0:T(8,128)(2,1)S(1)}, bf16[128,1024]{1,0:T(8,128)(2,1)}, u32[]{:S(2)}) copy-start(bf16[128,1024]{1,0:T(8,128)(2,1)} %param.4) | copy-start | bytes 786436
  0.0 1.4 %copy-start.5 = (bf16[128,1024]{1,0:T(8,128)(2,1)S(1)}, bf16[128,1024]{1,0:T(8,128)(2,1)}, u32[]{:S(2)}) copy-start(bf16[128,1024]{1,0:T(8,128)(2,1)} %param.5) | copy-start | bytes 786436
  26.6 29.9 %copy-start.1 = (bf16[128,8,768]{2,0,1:T(8,128)(2,1)}, bf16[128,8,768]{2,0,1:T(8,128)(2,1)S(1)}, u32[]{:S(2)}) copy-start(bf16[128,8,768]{2,0,1:T(8,128)(2,1)S(1)} %all_to_all.34) | copy-start | bytes 4718596
  26.6 12.6 %collective-permute-start = (bf16[1024,256]{1,0:T(8,128)(2,1)S(1)}, bf16[1024,256]{1,0:T(8,128)(2,1)S(1)}, u32[]{:S(2)}, u32[]{:S(2)}) collective-permute-start(bf16[1024,256]{1,0:T(8,128)(2,1)S(1)} %slice.4), channel_id=1, source_target_pairs={{0,8},{8,16},{16,24},{24,32},{32,40},{40,48},{48,56},{56,64},{64,7... | collective-permute-start | bytes 1572872 | tf_op jit(solution)/shard_map/ppermute | solution.py:21
  39.2 24.3 %copy-start.2 = (bf16[1024,256]{1,0:T(8,128)(2,1)}, bf16[1024,256]{1,0:T(8,128)(2,1)S(1)}, u32[]{:S(2)}) copy-start(bf16[1024,256]{1,0:T(8,128)(2,1)S(1)} %collective-permute-done.kv_ref) | copy-start | bytes 1572868
  39.2 11.7 %collective-permute-start.1 = (bf16[1024,256]{1,0:T(8,128)(2,1)S(1)}, bf16[1024,256]{1,0:T(8,128)(2,1)S(1)}, u32[]{:S(2)}, u32[]{:S(2)}) collective-permute-start(bf16[1024,256]{1,0:T(8,128)(2,1)S(1)} %collective-permute-done.kv_ref), channel_id=1, source_target_pairs={{0,8},{8,16},{16,24},{24,32},{32,40},{40,48},{48,56},{56,64},{64,7... | collective-permute-start | bytes 1572872 | tf_op jit(solution)/shard_map/ppermute | solution.py:21
  50.9 20.6 %copy-start.4 = (bf16[1024,256]{1,0:T(8,128)(2,1)}, bf16[1024,256]{1,0:T(8,128)(2,1)S(1)}, u32[]{:S(2)}) copy-start(bf16[1024,256]{1,0:T(8,128)(2,1)S(1)} %collective-permute-done.1.kv_ref) | copy-start | bytes 1572868
  50.9 28.6 %collective-permute-start.2 = (bf16[1024,256]{1,0:T(8,128)(2,1)S(1)}, bf16[1024,256]{1,0:T(8,128)(2,1)S(1)}, u32[]{:S(2)}, u32[]{:S(2)}) collective-permute-start(bf16[1024,256]{1,0:T(8,128)(2,1)S(1)} %collective-permute-done.1.kv_ref), channel_id=1, source_target_pairs={{0,8},{8,16},{16,24},{24,32},{32,40},{40,48},{48,56},{56,64},{64,7... | collective-permute-start | bytes 1572872 | tf_op jit(solution)/shard_map/ppermute | solution.py:21
  79.5 0.8 copy-start.3
